TPU v7x, 128 devices: a whole 4x4x4 slice. The times are simulated.
128 devices in a mesh: grp: 8 (over y, core), shard: 16 (over z, x).
Axes of the slice: x: 4, y: 4, z: 4, core: 2. Of those that a mesh axis runs over, the one named last changes fastest.
Arguments:
- tokens: bfloat16 [65536, 2560], P(('grp', 'shard')), may hold values from -6 to 6
- gain: float32 [2560], replicated, may hold values from 0.25 to 1.75
- w_qkv: bfloat16 [2560, 3072], P(None, 'shard'), may hold values from -1 to 1
- prefix_kv: bfloat16 [8, 2048, 512], P('grp', 'shard'), may hold values from -6 to 6
- prefix_owner: int32 [8], P('grp'), may hold values from 0 to 7, as said below
- suffix_len: int32 [8, 16], P('grp', 'shard'), may hold values from 1 to 512, 5120 in all within a row
- slots: int32 [8, 8192], P('grp', 'shard'), may hold values from 0 to 8191, as said below
Outputs:
- attended: bfloat16 [65536, 2560], P(('grp', 'shard'))
Inputs may be any that keep to these rules, and one draw needn't show every extreme that they name: In each group the slots are a permutation of 0 to 8191; in each aligned run of 512 entries the k-th block of 32 entries holds slots k * 512 to (k + 1) * 512 - 1. `suffix_len`: each group's lengths sum to 5120 and one of them equals 512. `prefix_owner`: each entry names one of the 8 caches; several groups may name the same one.
All inputs are finite; a program needn't handle non-finite values.
Results may differ from a plain program's by a relative error of at most 0.0069.
Values may be sent and summed in bfloat16 or wider, within the bound.
No kernel may reach another device: no remote copies, remote signals or barrier semaphores. Data moves between devices by JAX's collectives and lax.ppermute only.
A program may use at most 128 MiB of HBM per device.

v0:
```python
import jax
import jax.numpy as jnp
from jax import lax
from jax.sharding import PartitionSpec as P

H = 10
HD = 256
WINDOW = 2048
SUF = 512
HQ = 2560


def normalize(rows, gain):
    rows32 = rows.astype(jnp.float32)
    factor = lax.rsqrt(jnp.mean(rows32 * rows32, axis=-1, keepdims=True) + 1e-06)
    return (rows32 * factor * gain).astype(jnp.bfloat16)


def attend_request(queries, suffix_kv, prefix, length):
    keys = jnp.concatenate([prefix[:, :HD], suffix_kv[:, :HD]], axis=0)
    values = jnp.concatenate([prefix[:, HD:], suffix_kv[:, HD:]], axis=0)
    span = keys.shape[0]
    prefix_len = prefix.shape[0]
    count = queries.shape[0]
    query_pos = jnp.arange(count, dtype=jnp.int32)[:, None]
    key_pos = jnp.arange(span, dtype=jnp.int32)[None, :]
    visible = (
        (key_pos > prefix_len + query_pos - WINDOW)
        & (key_pos <= prefix_len + query_pos)
        & (key_pos < prefix_len + length)
    )
    heads = queries.reshape(count, H, HD).transpose(1, 0, 2)

    def one_head(head_q):
        scores = jnp.dot(head_q, keys.T, preferred_element_type=jnp.float32) * HD ** (-0.5)
        scores = jnp.where(visible, scores, -1e30)
        top = jnp.max(scores, axis=-1, keepdims=True)
        expd = jnp.exp(scores - top)
        weights = (expd / jnp.sum(expd, axis=-1, keepdims=True)).astype(jnp.bfloat16)
        return jnp.dot(weights, values, preferred_element_type=jnp.float32)

    result = lax.map(one_head, heads).transpose(1, 0, 2).reshape(count, H * HD)
    return jnp.where(query_pos < length, result, 0.0).astype(jnp.bfloat16)


def gather_by_a2a(piece, axis_name, count):
    spread = jnp.broadcast_to(piece[None], (count,) + piece.shape)
    return lax.all_to_all(spread, axis_name, 0, 0, tiled=True)


def shards(tokens, gain, w_qkv, prefix_kv, prefix_owner, suffix_len, slots):
    tok_dev = tokens.shape[0]
    n_grp = lax.axis_size("grp")
    n_shard = lax.axis_size("shard")
    grp = lax.axis_index("grp")
    core = grp % 2
    pairs = [(g, g ^ 1) for g in range(n_grp)]
    normed = normalize(tokens, gain)
    partner_rows = lax.ppermute(normed, "grp", pairs)
    cols = w_qkv.shape[1]
    half = cols // 2
    w_mine = lax.dynamic_slice_in_dim(w_qkv, core * half, half, axis=1)
    w_gathered = lax.all_gather(w_mine, "shard", axis=1, tiled=True)
    both = jnp.concatenate([normed, partner_rows], axis=0)
    out = jnp.dot(both, w_gathered, preferred_element_type=jnp.float32).astype(jnp.bfloat16)
    out_mine = out[:tok_dev]
    out_back = lax.ppermute(out[tok_dev:], "grp", pairs)
    is0 = core == 0
    half0 = jnp.where(is0, out_mine, out_back).reshape(tok_dev, n_shard, 1, half)
    half1 = jnp.where(is0, out_back, out_mine).reshape(tok_dev, n_shard, 1, half)
    projected = jnp.concatenate([half0, half1], axis=2).reshape(tok_dev, n_shard * cols)
    order = slots.reshape(tok_dev)
    arrived, order = (
        lax.all_to_all(projected, "shard", split_axis=0, concat_axis=0, tiled=True),
        lax.all_to_all(order, "shard", split_axis=0, concat_axis=0, tiled=True),
    )
    first_slot = lax.axis_index("shard") * tok_dev
    pos = order - first_slot
    onehot = (jnp.arange(tok_dev, dtype=jnp.int32)[:, None] == pos[None, :]).astype(jnp.bfloat16)
    placed = jnp.dot(onehot, arrived, preferred_element_type=jnp.float32).astype(jnp.bfloat16)
    owner = prefix_owner[0]
    sliced = gather_by_a2a(prefix_kv[0], "grp", n_grp)
    chosen = lax.dynamic_index_in_dim(sliced, owner, 0, keepdims=False)
    prefix = gather_by_a2a(chosen, "shard", n_shard).reshape(-1, chosen.shape[-1])
    lengths = suffix_len.reshape(-1)
    results = attend_request(placed[:, :HQ], placed[:, HQ:], prefix, lengths[0])
    return results


def solution(mesh):
    return jax.shard_map(
        shards,
        mesh=mesh,
        in_specs=(
            P(("grp", "shard"), None),
            P(),
            P(None, "shard"),
            P("grp", "shard", None),
            P("grp"),
            P("grp", "shard"),
            P("grp", "shard"),
        ),
        out_specs=P(("grp", "shard"), None),
        check_vma=False,
    )
```

profile of v0, /device:TPU:0, one launch (start us, length us, event | category | flops | bytes accessed | tf_op | source)
XLA Modules:
  0.0 301.8 jit_solution(2866371976029989938)
XLA Ops:
  6.5 1.2 copy-done
  7.7 0.8 constant_dynamic-slice_fusion
  8.6 2.5 fusion.11
  11.1 2.2 fusion.13
  13.3 1.1 broadcast_in_dim.49
  14.3 4.7 %all-to-all-start.2 = ((bf16[8,128,512]{2,1,0:T(8,128)(2,1)}), bf16[8,128,512]{2,1,0:T(8,128)(2,1)S(1)}, u32[]{:S(2)}, u32[]{:S(2)}) async-start(bf16[8,128,512]{2,1,0:T(8,128)(2,1)} %broadcast_in_dim.49), calls=%async_computation.2 | async-start | bytes 2097152 | tf_op jit(solution)/shard_map/all_to_all | solution.py:48
  19.0 61.6 %all-gather.2.cloned.1.call-done = bf16[2560,1536]{0,1:T(8,128)(2,1)} async-done(((bf16[2560,96]{0,1:T(8,128)(2,1)}), bf16[2560,1536]{0,1:T(8,128)(2,1)}) %all-gather.2.cloned.1.call-update) | async-done | bytes 7864336 | tf_op jit(solution)/shard_map/all_gather | solution.py:63
  80.6 12.2 %fusion.19 = bf16[1024,1536]{1,0:T(8,128)(2,1)S(1)} fusion(bf16[2560,1536]{0,1:T(8,128)(2,1)} %all-gather.2.cloned.1.call-done, bf16[512,2560]{1,0:T(8,128)(2,1)} %collective-permute-done, bf16[512,2560]{1,0:T(8,128)(2,1)} %fusion.13), kind=kOutput, calls=%fused_computation.27 | convolution fusion | flops 8065122304 | bytes 16252928 | tf_op jit(solution)/shard_map/dot_general | solution.py:65
  92.9 1.6 copy-done.5
  94.5 1.3 slice.32
  95.8 0.5 broadcast.60
  96.3 0.7 reduce.7
  97.0 0.7 all_to_all.20
  98.3 5.3 %all-to-all-start = ((s32[16,32,1]{1,2,0:T(1,128)}), s32[16,32,1]{1,2,0:T(1,128)S(1)}, u32[]{:S(2)}, u32[]{:S(2)}) async-start(s32[16,32,1]{1,2,0:T(1,128)} %all_to_all.20), calls=%async_computation | async-start | bytes 16384 | tf_op jit(solution)/shard_map/all_to_all | solution.py:75
  103.6 7.5 %all-to-all-done = s32[16,32,1]{1,2,0:T(1,128)S(1)} async-done(((s32[16,32,1]{1,2,0:T(1,128)}), s32[16,32,1]{1,2,0:T(1,128)S(1)}, u32[]{:S(2)}, u32[]{:S(2)}) %all-to-all-start) | async-done | bytes 2080 | tf_op jit(solution)/shard_map/all_to_all | solution.py:75
  111.1 1.5 broadcast_in_dim.51
  112.6 3.7 %all-to-all-start.3 = ((bf16[16,128,512]{2,1,0:T(8,128)(2,1)}), bf16[16,128,512]{2,1,0:T(8,128)(2,1)S(1)}, u32[]{:S(2)}, u32[]{:S(2)}) async-start(bf16[16,128,512]{2,1,0:T(8,128)(2,1)} %broadcast_in_dim.51), calls=%async_computation.3 | async-start | bytes 4194304 | tf_op jit(solution)/shard_map/all_to_all | solution.py:48
  116.4 3.8 %broadcast_select_fusion.1 = (bf16[512,1536]{1,0:T(8,128)(2,1)}, bf16[512,1536]{1,0:T(8,128)(2,1)}) fusion(bf16[512,1536]{1,0:T(8,128)(2,1)} %collective-permute-done.1, pred[]{:T(512)S(6)} %eq.21, bf16[1024,1536]{1,0:T(8,128)(2,1)} %copy-done.5), kind=kLoop, calls=%fused_computation.30 | loop fusion | flops 1572864 | bytes 6291457 | tf_op jit(solution)/shard_map/jit(_where)/select_n | solution.py:69
  120.1 2.6 copy.17
  122.7 2.6 copy.18
  125.3 3.9 %pad_maximum_fusion = bf16[512,16,2,96]{0,3,1,2:T(8,128)(2,1)} fusion(bf16[512,16,1,96]{0,3,1,2:T(8,128)(2,1)} %bitcast.48, bf16[512,16,1,96]{0,3,1,2:T(8,128)(2,1)} %bitcast.47), kind=kLoop, calls=%fused_computation.28 | loop fusion | flops 1572864 | bytes 6291456 | tf_op jit(solution)/shard_map/concatenate | solution.py:71
  129.2 11.2 %copy.19 = bf16[512,16,2,96]{3,2,1,0:T(2,128)(2,1)} copy(bf16[512,16,2,96]{0,3,1,2:T(8,128)(2,1)} %pad_maximum_fusion) | data formatting | bytes 6291456 | tf_op jit(solution)/shard_map/concatenate | solution.py:71
  140.4 12.4 %all_to_all.22 = bf16[16,32,3072]{2,1,0:T(8,128)(2,1)} reshape(bf16[512,16,2,96]{3,2,1,0:T(2,128)(2,1)} %copy.19) | data formatting | bytes 6291456 | tf_op jit(solution)/shard_map/all_to_all | solution.py:74
  152.8 7.2 %all-to-all-start.1 = ((bf16[16,32,3072]{2,1,0:T(8,128)(2,1)}), bf16[16,32,3072]{2,1,0:T(8,128)(2,1)}, u32[]{:S(2)}, u32[]{:S(2)}) async-start(bf16[16,32,3072]{2,1,0:T(8,128)(2,1)} %all_to_all.22), calls=%async_computation.1 | async-start | bytes 6291456 | tf_op jit(solution)/shard_map/all_to_all | solution.py:74
  160.8 1.5 fusion.26
  162.4 42.2 %all-to-all-done.1 = bf16[16,32,3072]{2,1,0:T(8,128)(2,1)} async-done(((bf16[16,32,3072]{2,1,0:T(8,128)(2,1)}), bf16[16,32,3072]{2,1,0:T(8,128)(2,1)}, u32[]{:S(2)}, u32[]{:S(2)}) %all-to-all-start.1) | async-done | bytes 3145760 | tf_op jit(solution)/shard_map/all_to_all | solution.py:74
  204.6 3.7 %convolution_convert_fusion = bf16[512,3072]{1,0:T(8,128)(2,1)S(1)} fusion(bf16[512,3072]{1,0:T(8,128)(2,1)} %bitcast.3, s32[512]{0:T(512)S(1)} %sub.24), kind=kOutput, calls=%fused_computation.26 | convolution fusion | flops 1612447744 | bytes 6293504 | tf_op jit(solution)/shard_map/dot_general | solution.py:80
  208.3 1.7 slice.33
  210.0 4.6 %copy.20 = bf16[512,2560]{0,1:T(8,128)(2,1)} copy(bf16[512,2560]{1,0:T(8,128)(2,1)} %slice.33) | data formatting | bytes 5242880 | tf_op jit(solution)/shard_map/slice | solution.py:86
  214.6 1.7 pad_maximum_fusion.1
  216.3 70.5 %while.11 = (s32[]{:T(128)}, bf16[10,512,256]{1,2,0:T(8,128)(2,1)}, bf16[10,512,256]{1,2,0:T(8,128)(2,1)}, bf16[2560,256]{1,0:T(8,128)(2,1)}, bf16[2560,256]{1,0...) while((s32[]{:T(128)}, bf16[10,512,256]{1,2,0:T(8,128)(2,1)}, ...), condition=%wide.region_4.5_spmd.clone, body=%wide.region_1.4_spmd.clone.sunk | while | flops 1357904896 | bytes 24395376 | solution.py:42
  216.3 3.7 %fusion.38 = (f32[512]{0:T(512)S(1)}, f32[512,2560]{1,0:T(8,128)S(1)}) fusion(bf16[2560,256]{1,0:T(8,128)(2,1)} %get-tuple-element.160, bf16[10,512,256]{1,2,0:T(8,128)(2,1)} %get-tuple-element.159, s32[]{:T(128)} %get-tuple-element.149, pred[2560]{0:T(1024)(128)(4,1)S(1)} %get-tuple-element.163, s32[512]{0:T(512)S(1)} %get-tuple-element.162), kind=kOutput, calls=%fused_computation.43.clone.1 | convolution fusion | flops 680263168 | bytes 6822912 | tf_op jit(solution)/shard_map/while/body/eval_jaxpr/dot_general | solution.py:35
  220.0 0.8 fusion.39
  221.3 2.0 fusion.40
  223.3 3.7 %fusion.38 = (f32[512]{0:T(512)S(1)}, f32[512,2560]{1,0:T(8,128)S(1)}) fusion(bf16[2560,256]{1,0:T(8,128)(2,1)} %get-tuple-element.160, bf16[10,512,256]{1,2,0:T(8,128)(2,1)} %get-tuple-element.159, s32[]{:T(128)} %get-tuple-element.149, pred[2560]{0:T(1024)(128)(4,1)S(1)} %get-tuple-element.163, s32[512]{0:T(512)S(1)} %get-tuple-element.162), kind=kOutput, calls=%fused_computation.43.clone.1 | convolution fusion | flops 680263168 | bytes 6822912 | tf_op jit(solution)/shard_map/while/body/eval_jaxpr/dot_general | solution.py:35
  227.0 0.8 fusion.39
  227.9 0.5 copy-done.6
  228.3 2.0 fusion.40
  230.4 3.7 %fusion.38 = (f32[512]{0:T(512)S(1)}, f32[512,2560]{1,0:T(8,128)S(1)}) fusion(bf16[2560,256]{1,0:T(8,128)(2,1)} %get-tuple-element.160, bf16[10,512,256]{1,2,0:T(8,128)(2,1)} %get-tuple-element.159, s32[]{:T(128)} %get-tuple-element.149, pred[2560]{0:T(1024)(128)(4,1)S(1)} %get-tuple-element.163, s32[512]{0:T(512)S(1)} %get-tuple-element.162), kind=kOutput, calls=%fused_computation.43.clone.1 | convolution fusion | flops 680263168 | bytes 6822912 | tf_op jit(solution)/shard_map/while/body/eval_jaxpr/dot_general | solution.py:35
  234.1 0.8 fusion.39
  235.4 2.0 fusion.40
  237.4 3.7 %fusion.38 = (f32[512]{0:T(512)S(1)}, f32[512,2560]{1,0:T(8,128)S(1)}) fusion(bf16[2560,256]{1,0:T(8,128)(2,1)} %get-tuple-element.160, bf16[10,512,256]{1,2,0:T(8,128)(2,1)} %get-tuple-element.159, s32[]{:T(128)} %get-tuple-element.149, pred[2560]{0:T(1024)(128)(4,1)S(1)} %get-tuple-element.163, s32[512]{0:T(512)S(1)} %get-tuple-element.162), kind=kOutput, calls=%fused_computation.43.clone.1 | convolution fusion | flops 680263168 | bytes 6822912 | tf_op jit(solution)/shard_map/while/body/eval_jaxpr/dot_general | solution.py:35
  241.1 0.8 fusion.39
  242.4 2.0 fusion.40
  244.5 3.7 %fusion.38 = (f32[512]{0:T(512)S(1)}, f32[512,2560]{1,0:T(8,128)S(1)}) fusion(bf16[2560,256]{1,0:T(8,128)(2,1)} %get-tuple-element.160, bf16[10,512,256]{1,2,0:T(8,128)(2,1)} %get-tuple-element.159, s32[]{:T(128)} %get-tuple-element.149, pred[2560]{0:T(1024)(128)(4,1)S(1)} %get-tuple-element.163, s32[512]{0:T(512)S(1)} %get-tuple-element.162), kind=kOutput, calls=%fused_computation.43.clone.1 | convolution fusion | flops 680263168 | bytes 6822912 | tf_op jit(solution)/shard_map/while/body/eval_jaxpr/dot_general | solution.py:35
  248.2 0.8 fusion.39
  249.5 2.0 fusion.40
  251.5 3.7 %fusion.38 = (f32[512]{0:T(512)S(1)}, f32[512,2560]{1,0:T(8,128)S(1)}) fusion(bf16[2560,256]{1,0:T(8,128)(2,1)} %get-tuple-element.160, bf16[10,512,256]{1,2,0:T(8,128)(2,1)} %get-tuple-element.159, s32[]{:T(128)} %get-tuple-element.149, pred[2560]{0:T(1024)(128)(4,1)S(1)} %get-tuple-element.163, s32[512]{0:T(512)S(1)} %get-tuple-element.162), kind=kOutput, calls=%fused_computation.43.clone.1 | convolution fusion | flops 680263168 | bytes 6822912 | tf_op jit(solution)/shard_map/while/body/eval_jaxpr/dot_general | solution.py:35
  255.2 0.8 fusion.39
  256.5 2.0 fusion.40
  258.5 3.7 %fusion.38 = (f32[512]{0:T(512)S(1)}, f32[512,2560]{1,0:T(8,128)S(1)}) fusion(bf16[2560,256]{1,0:T(8,128)(2,1)} %get-tuple-element.160, bf16[10,512,256]{1,2,0:T(8,128)(2,1)} %get-tuple-element.159, s32[]{:T(128)} %get-tuple-element.149, pred[2560]{0:T(1024)(128)(4,1)S(1)} %get-tuple-element.163, s32[512]{0:T(512)S(1)} %get-tuple-element.162), kind=kOutput, calls=%fused_computation.43.clone.1 | convolution fusion | flops 680263168 | bytes 6822912 | tf_op jit(solution)/shard_map/while/body/eval_jaxpr/dot_general | solution.py:35
  262.3 0.8 fusion.39
  263.6 2.0 fusion.40
  265.6 3.7 %fusion.38 = (f32[512]{0:T(512)S(1)}, f32[512,2560]{1,0:T(8,128)S(1)}) fusion(bf16[2560,256]{1,0:T(8,128)(2,1)} %get-tuple-element.160, bf16[10,512,256]{1,2,0:T(8,128)(2,1)} %get-tuple-element.159, s32[]{:T(128)} %get-tuple-element.149, pred[2560]{0:T(1024)(128)(4,1)S(1)} %get-tuple-element.163, s32[512]{0:T(512)S(1)} %get-tuple-element.162), kind=kOutput, calls=%fused_computation.43.clone.1 | convolution fusion | flops 680263168 | bytes 6822912 | tf_op jit(solution)/shard_map/while/body/eval_jaxpr/dot_general | solution.py:35
  269.3 0.8 fusion.39
  270.6 2.0 fusion.40
  272.6 3.7 %fusion.38 = (f32[512]{0:T(512)S(1)}, f32[512,2560]{1,0:T(8,128)S(1)}) fusion(bf16[2560,256]{1,0:T(8,128)(2,1)} %get-tuple-element.160, bf16[10,512,256]{1,2,0:T(8,128)(2,1)} %get-tuple-element.159, s32[]{:T(128)} %get-tuple-element.149, pred[2560]{0:T(1024)(128)(4,1)S(1)} %get-tuple-element.163, s32[512]{0:T(512)S(1)} %get-tuple-element.162), kind=kOutput, calls=%fused_computation.43.clone.1 | convolution fusion | flops 680263168 | bytes 6822912 | tf_op jit(solution)/shard_map/while/body/eval_jaxpr/dot_general | solution.py:35
  276.4 0.8 fusion.39
  277.7 2.0 fusion.40
  279.7 3.7 %fusion.38 = (f32[512]{0:T(512)S(1)}, f32[512,2560]{1,0:T(8,128)S(1)}) fusion(bf16[2560,256]{1,0:T(8,128)(2,1)} %get-tuple-element.160, bf16[10,512,256]{1,2,0:T(8,128)(2,1)} %get-tuple-element.159, s32[]{:T(128)} %get-tuple-element.149, pred[2560]{0:T(1024)(128)(4,1)S(1)} %get-tuple-element.163, s32[512]{0:T(512)S(1)} %get-tuple-element.162), kind=kOutput, calls=%fused_computation.43.clone.1 | convolution fusion | flops 680263168 | bytes 6822912 | tf_op jit(solution)/shard_map/while/body/eval_jaxpr/dot_general | solution.py:35
  283.4 0.8 fusion.39
  284.7 2.0 fusion.40
  286.7 3.8 %fusion.18 = bf16[512,2560]{0,1:T(8,128)(2,1)} fusion(bf16[10,512,256]{1,2,0:T(8,128)(2,1)} %get-tuple-element.37, pred[512]{0:T(512)(128)(4,1)S(1)} %iota_compare_fusion.5), kind=kLoop, calls=%fused_computation.25 | loop fusion | flops 1310720 | bytes 5243392 | tf_op jit(solution)/shard_map/convert_element_type | solution.py:43
  290.5 4.4 %copy.23 = bf16[512,2560]{1,0:T(8,128)(2,1)} copy(bf16[512,2560]{0,1:T(8,128)(2,1)} %fusion.18) | data formatting | bytes 5242880 | tf_op jit(solution)/shard_map/convert_element_type | solution.py:43
  (52 shorter events, 4.6 us)
Async XLA Ops:
  6.5 1.2 copy-start
  6.5 4.5 %copy-start.8 = (f32[2560]{0:T(1024)S(1)}, f32[2560]{0:T(1024)}, u32[]{:S(2)}) copy-start(f32[2560]{0:T(1024)} %param.10) | copy-start | bytes 30724
  6.5 74.1 %all-gather.2.cloned.1.call-start = ((), (), s32[]{:S(2)}) async-start(), calls=%async_computation.4 | async-start | bytes 8355840 | tf_op jit(solution)/shard_map/all_gather | solution.py:63
  8.6 2.5 copy-start.2
  11.1 2.2 copy-start.7
  13.3 5.8 %collective-permute-start = (bf16[512,2560]{1,0:T(8,128)(2,1)}, bf16[512,2560]{1,0:T(8,128)(2,1)}, u32[]{:S(2)}, u32[]{:S(2)}) collective-permute-start(bf16[512,2560]{1,0:T(8,128)(2,1)} %fusion.13), channel_id=1, source_target_pairs={{0,16},{16,0},{32,48},{48,32},{64,80},{80,64},{96,112},{112,96},{1... | collective-permute-start | bytes 7864328 | tf_op jit(solution)/shard_map/ppermute | solution.py:59
  14.3 84.0 %all-to-all-start.2 = ((bf16[8,128,512]{2,1,0:T(8,128)(2,1)}), bf16[8,128,512]{2,1,0:T(8,128)(2,1)S(1)}, u32[]{:S(2)}, u32[]{:S(2)}) async-start(bf16[8,128,512]{2,1,0:T(8,128)(2,1)} %broadcast_in_dim.49), calls=%async_computation.2 | async-start | bytes 2097152 | tf_op jit(solution)/shard_map/all_to_all | solution.py:48
  92.9 1.6 copy-start.5
  94.5 1.8 copy-start.9
  95.8 20.6 %collective-permute-start.1 = (bf16[512,1536]{1,0:T(8,128)(2,1)}, bf16[512,1536]{1,0:T(8,128)(2,1)}, u32[]{:S(2)}, u32[]{:S(2)}) collective-permute-start(bf16[512,1536]{1,0:T(8,128)(2,1)} %slice.32), channel_id=1, source_target_pairs={{0,16},{16,0},{32,48},{48,32},{64,80},{80,64},{96,112},{112,96},{1... | collective-permute-start | bytes 4718600 | tf_op jit(solution)/shard_map/ppermute | solution.py:67
  98.3 12.8 %all-to-all-start = ((s32[16,32,1]{1,2,0:T(1,128)}), s32[16,32,1]{1,2,0:T(1,128)S(1)}, u32[]{:S(2)}, u32[]{:S(2)}) async-start(s32[16,32,1]{1,2,0:T(1,128)} %all_to_all.20), calls=%async_computation | async-start | bytes 16384 | tf_op jit(solution)/shard_map/all_to_all | solution.py:75
  112.6 40.2 %all-to-all-start.3 = ((bf16[16,128,512]{2,1,0:T(8,128)(2,1)}), bf16[16,128,512]{2,1,0:T(8,128)(2,1)S(1)}, u32[]{:S(2)}, u32[]{:S(2)}) async-start(bf16[16,128,512]{2,1,0:T(8,128)(2,1)} %broadcast_in_dim.51), calls=%async_computation.3 | async-start | bytes 4194304 | tf_op jit(solution)/shard_map/all_to_all | solution.py:48
  152.8 51.8 %all-to-all-start.1 = ((bf16[16,32,3072]{2,1,0:T(8,128)(2,1)}), bf16[16,32,3072]{2,1,0:T(8,128)(2,1)}, u32[]{:S(2)}, u32[]{:S(2)}) async-start(bf16[16,32,3072]{2,1,0:T(8,128)(2,1)} %all_to_all.22), calls=%async_computation.1 | async-start | bytes 6291456 | tf_op jit(solution)/shard_map/all_to_all | solution.py:74
  210.0 4.6 %copy-start.3 = (bf16[2048,256]{1,0:T(8,128)(2,1)S(1)}, bf16[2048,256]{1,0:T(8,128)(2,1)}, u32[]{:S(2)}) copy-start(bf16[2048,256]{1,0:T(8,128)(2,1)} %get-tuple-element.90) | copy-start | bytes 3145732
  210.0 4.6 %copy-start.4 = (bf16[2048,256]{1,0:T(8,128)(2,1)S(1)}, bf16[2048,256]{1,0:T(8,128)(2,1)}, u32[]{:S(2)}) copy-start(bf16[2048,256]{1,0:T(8,128)(2,1)} %get-tuple-element.91) | copy-start | bytes 3145732
  220.0 1.3 copy-start.6
  227.0 1.3 copy-start.6
  234.1 1.3 copy-start.6
  241.1 1.3 copy-start.6
  248.2 1.3 copy-start.6
  255.2 1.3 copy-start.6
  262.2 1.3 copy-start.6
  269.3 1.3 copy-start.6
  276.3 1.3 copy-start.6
  283.4 1.3 copy-start.6
  286.7 8.2 %copy-start.1 = (bf16[2560,192]{0,1:T(8,128)(2,1)S(1)}, bf16[2560,192]{0,1:T(8,128)(2,1)}, u32[]{:S(2)}) copy-start(bf16[2560,192]{0,1:T(8,128)(2,1)} %param.11) | copy-start | bytes 2949124
Sparse Core Ops, SparseCore 0:
  9.5 71.1 all-gather.1
where the time goes:
time: 303 us; the launch traced here: 302 us
  waiting for transfers between devices  111 us (37%)
  matrix products  73.1 us (24%)
  local copies, waits for them, and re-layouts  54.7 us (18%)
  other arithmetic  26.8 us (9%)
  starting transfers between devices  20.9 us (7%)
  between operations  14.9 us (5%)
    all_gather x1, waiting for transfers between devices, shards(): w_gathered = lax.all_gather(w_mine, 'shard', axis=1, tiled=True)  61.6 us
    all_to_all x1, waiting for transfers between devices, shards(): lax.all_to_all(projected, 'shard', split_axis=0, concat_axis=0, tiled=True)  42.2 us
    dot_general x10, matrix products, one_head(): jnp.dot(head_q, keys.T, preferred_element_type=jnp.float32) * HD ** (-0.5)  37 us
    dot_general x10, matrix products, one_head(): return jnp.dot(weights, values, preferred_element_type=jnp.float32)  20.2 us
    all_to_all x1, local copies, waits for them, and re-layouts, shards(): lax.all_to_all(projected, 'shard', split_axis=0, concat_axis=0, tiled=True)  12.4 us
    dot_general x1, matrix products, shards(): jnp.dot(both, w_gathered, preferred_element_type=jnp.float32)  12.2 us
    concatenate x1, local copies, waits for them, and re-layouts, shards(): jnp.concatenate([half0, half1], axis=2).reshape(tok_dev, n_shard * cols)  11.2 us
    all_to_all x2, starting transfers between devices, gather_by_a2a(): return lax.all_to_all(spread, axis_name, 0, 0, tiled=True)  8.41 us
  transfers between devices with their start and end apart: 7, of which 3 were waited for; matrix products, arithmetic and copies ran while one was open for 16% of the time, Pallas kernels for 0%

commit v1 on v0

--- a/solution.py
+++ b/solution.py
@@ -60,7 +60,23 @@
     cols = w_qkv.shape[1]
     half = cols // 2
     w_mine = lax.dynamic_slice_in_dim(w_qkv, core * half, half, axis=1)
-    w_gathered = lax.all_gather(w_mine, "shard", axis=1, tiled=True)
+    ways, here, step = (lax.axis_size("shard"), lax.axis_index("shard"), w_mine.shape[1])
+    dims = [n * ways if d == 1 else n for d, n in enumerate(w_mine.shape)]
+    full = lax.dynamic_update_slice_in_dim(
+        jnp.zeros(dims, w_mine.dtype), w_mine, here * step, axis=1
+    )
+    going_up = going_down = w_mine
+    for far in range(1, ways // 2 + 1):
+        going_up = lax.ppermute(going_up, "shard", [(d, (d + 1) % ways) for d in range(ways)])
+        full = lax.dynamic_update_slice_in_dim(full, going_up, (here - far) % ways * step, axis=1)
+        if 2 * far < ways:
+            going_down = lax.ppermute(
+                going_down, "shard", [(d, (d - 1) % ways) for d in range(ways)]
+            )
+            full = lax.dynamic_update_slice_in_dim(
+                full, going_down, (here + far) % ways * step, axis=1
+            )
+    w_gathered = full
     both = jnp.concatenate([normed, partner_rows], axis=0)
     out = jnp.dot(both, w_gathered, preferred_element_type=jnp.float32).astype(jnp.bfloat16)
     out_mine = out[:tok_dev]

time: 303 us -> 310 us (1.023)
  starting transfers between devices: 20.9 us -> 54.9 us
  between operations: 14.9 us -> 1.52 us
  matrix products: 73.1 us -> 64.3 us
  other arithmetic: 26.8 us -> 21.7 us
  waiting for transfers between devices: 111 us -> 106 us
  local copies, waits for them, and re-layouts: 54.7 us -> 59.5 us
    all_gather x1 -> x0, waiting for transfers between devices: 61.6 us -> none  [shards(): w_gathered = lax.all_gather(w_mine, 'shard', axis=1, tiled=True)]
    ppermute x0 -> x15, waiting for transfers between devices: none -> 53.2 us  [the longest x8 53.2 us: shards(): lax.ppermute(going_up, 'shard', [(d, (d + 1) % ways) for d in range(ways)])]
    ppermute x0 -> x15, starting transfers between devices: none -> 38.4 us  [the longest x7 36.8 us: shards(): lax.ppermute(going_down, 'shard', [(d, (d - 1) % ways) for d in range(way...]
    dynamic_update_slice x0 -> x16, local copies, waits for them, and re-layouts: none -> 14.3 us  [the longest x8 7.58 us: shards(): lax.dynamic_update_slice_in_dim(full, going_up, (here - far) % ways * ste...]
    dot_general x10, matrix products: 20.2 us -> 13.2 us  [one_head(): return jnp.dot(weights, values, preferred_element_type=jnp.float32)]
    all_to_all x2, waiting for transfers between devices: 0.01 us -> 3.51 us  [gather_by_a2a(): return lax.all_to_all(spread, axis_name, 0, 0, tiled=True)]
    all_to_all x1, starting transfers between devices: 7.2 us -> 3.74 us  [shards(): lax.all_to_all(projected, 'shard', split_axis=0, concat_axis=0, tiled=True)]
    slice x2, local copies, waits for them, and re-layouts: 6.25 us -> 2.82 us  [shards(): results = attend_request(placed[:, :HQ], placed[:, HQ:], prefix, lengths[0])]
  transfers between devices with their start and end apart: 7 -> 21, of which waited for: 3 -> 11; matrix products, arithmetic and copies ran while one was open for 16% -> 16% of each run, Pallas kernels for 0% -> 0%
where the time goes in v1:
time: 310 us; the launch traced here: 309 us
  waiting for transfers between devices  106 us (34%)
  matrix products  64.3 us (21%)
  local copies, waits for them, and re-layouts  59.5 us (19%)
  starting transfers between devices  54.9 us (18%)
  other arithmetic  21.7 us (7%)
    ppermute x8, waiting for transfers between devices, shards(): lax.ppermute(going_up, 'shard', [(d, (d + 1) % ways) for d in range(ways)])  53.2 us
    all_to_all x1, waiting for transfers between devices, shards(): lax.all_to_all(projected, 'shard', split_axis=0, concat_axis=0, tiled=True)  42.2 us
    dot_general x10, matrix products, one_head(): jnp.dot(head_q, keys.T, preferred_element_type=jnp.float32) * HD ** (-0.5)  37 us
    ppermute x7, starting transfers between devices, shards(): lax.ppermute(going_down, 'shard', [(d, (d - 1) % ways) for d in range(way...  36.8 us
    dot_general x10, matrix products, one_head(): return jnp.dot(weights, values, preferred_element_type=jnp.float32)  13.2 us
    all_to_all x1, local copies, waits for them, and re-layouts, shards(): lax.all_to_all(projected, 'shard', split_axis=0, concat_axis=0, tiled=True)  12.4 us
    dot_general x1, matrix products, shards(): jnp.dot(both, w_gathered, preferred_element_type=jnp.float32)  12.2 us
    all_to_all x2, starting transfers between devices, gather_by_a2a(): return lax.all_to_all(spread, axis_name, 0, 0, tiled=True)  9.2 us
  transfers between devices with their start and end apart: 21, of which 11 were waited for; matrix products, arithmetic and copies ran while one was open for 16% of the time, Pallas kernels for 0%

profile of v1, /device:TPU:0, one launch (start us, length us, event | category | flops | bytes accessed | tf_op | source)
XLA Modules:
  0.0 308.6 jit_solution(12268934104127682869)
XLA Ops:
  1.4 0.9 constant_dynamic-update-slice_fusion.15
  2.2 1.6 collective-permute-start.1
  3.8 4.7 %collective-permute-start.2 = (bf16[2560,96]{0,1:T(8,128)(2,1)}, bf16[2560,96]{0,1:T(8,128)(2,1)S(1)}, u32[]{:S(2)}, u32[]{:S(2)}) collective-permute-start(bf16[2560,96]{0,1:T(8,128)(2,1)} %get-tuple-element.85), channel_id=1, source_target_pairs={{0,15},{1,0},{2,1},{3,2},{4,3},{5,4},{6,5},{7,6},{8,7},{9,8},{10,9... | collective-permute-start | bytes 1474568 | tf_op jit(solution)/shard_map/ppermute | solution.py:73
  9.2 2.2 fusion.13
  11.4 1.1 broadcast_in_dim.53
  12.4 4.6 %all-to-all-start.2 = ((bf16[8,128,512]{2,1,0:T(8,128)(2,1)}), bf16[8,128,512]{2,1,0:T(8,128)(2,1)S(1)}, u32[]{:S(2)}, u32[]{:S(2)}) async-start(bf16[8,128,512]{2,1,0:T(8,128)(2,1)} %broadcast_in_dim.53), calls=%async_computation.2 | async-start | bytes 2097152 | tf_op jit(solution)/shard_map/all_to_all | solution.py:48
  17.0 3.1 %collective-permute-done.1 = bf16[2560,96]{0,1:T(8,128)(2,1)} collective-permute-done((bf16[2560,96]{0,1:T(8,128)(2,1)}, bf16[2560,96]{0,1:T(8,128)(2,1)}, u32[]{:S(2)}, u32[]{:S(2)}) %collective-permute-start.1) | collective-permute-done | bytes 491552 | tf_op jit(solution)/shard_map/ppermute | solution.py:70
  20.1 5.3 %collective-permute-start.4 = (bf16[2560,96]{0,1:T(8,128)(2,1)S(1)}, bf16[2560,96]{0,1:T(8,128)(2,1)S(1)}, u32[]{:S(2)}, u32[]{:S(2)}) collective-permute-start(bf16[2560,96]{0,1:T(8,128)(2,1)S(1)} %collective-permute-done.2), channel_id=1, source_target_pairs={{0,15},{1,0},{2,1},{3,2},{4,3},{5,4},{6,5},{7,6},{8,7},{9,8},{10,9... | collective-permute-start | bytes 1474568 | tf_op jit(solution)/shard_map/ppermute | solution.py:73
  25.5 1.8 constant_dynamic-update-slice_fusion.14
  28.1 7.9 %collective-permute-done.3 = bf16[2560,96]{0,1:T(8,128)(2,1)S(1)} collective-permute-done((bf16[2560,96]{0,1:T(8,128)(2,1)}, bf16[2560,96]{0,1:T(8,128)(2,1)S(1)}, u32[]{:S(2)}, u32[]{:S(2)}) %collective-permute-start.3) | collective-permute-done | bytes 491552 | tf_op jit(solution)/shard_map/ppermute | solution.py:70
  36.0 5.3 %collective-permute-start.6 = (bf16[2560,96]{0,1:T(8,128)(2,1)S(1)}, bf16[2560,96]{0,1:T(8,128)(2,1)S(1)}, u32[]{:S(2)}, u32[]{:S(2)}) collective-permute-start(bf16[2560,96]{0,1:T(8,128)(2,1)S(1)} %collective-permute-done.4), channel_id=1, source_target_pairs={{0,15},{1,0},{2,1},{3,2},{4,3},{5,4},{6,5},{7,6},{8,7},{9,8},{10,9... | collective-permute-start | bytes 1474568 | tf_op jit(solution)/shard_map/ppermute | solution.py:73
  43.0 7.9 %collective-permute-done.5 = bf16[2560,96]{0,1:T(8,128)(2,1)S(1)} collective-permute-done((bf16[2560,96]{0,1:T(8,128)(2,1)S(1)}, bf16[2560,96]{0,1:T(8,128)(2,1)S(1)}, u32[]{:S(2)}, u32[]{:S(2)}) %collective-permute-start.5) | collective-permute-done | bytes 491552 | tf_op jit(solution)/shard_map/ppermute | solution.py:70
  50.9 5.3 %collective-permute-start.8 = (bf16[2560,96]{0,1:T(8,128)(2,1)S(1)}, bf16[2560,96]{0,1:T(8,128)(2,1)S(1)}, u32[]{:S(2)}, u32[]{:S(2)}) collective-permute-start(bf16[2560,96]{0,1:T(8,128)(2,1)S(1)} %collective-permute-done.6), channel_id=1, source_target_pairs={{0,15},{1,0},{2,1},{3,2},{4,3},{5,4},{6,5},{7,6},{8,7},{9,8},{10,9... | collective-permute-start | bytes 1474568 | tf_op jit(solution)/shard_map/ppermute | solution.py:73
  57.9 7.0 %collective-permute-done.7 = bf16[2560,96]{0,1:T(8,128)(2,1)S(1)} collective-permute-done((bf16[2560,96]{0,1:T(8,128)(2,1)S(1)}, bf16[2560,96]{0,1:T(8,128)(2,1)S(1)}, u32[]{:S(2)}, u32[]{:S(2)}) %collective-permute-start.7) | collective-permute-done | bytes 491552 | tf_op jit(solution)/shard_map/ppermute | solution.py:70
  64.9 5.3 %collective-permute-start.10 = (bf16[2560,96]{0,1:T(8,128)(2,1)S(1)}, bf16[2560,96]{0,1:T(8,128)(2,1)S(1)}, u32[]{:S(2)}, u32[]{:S(2)}) collective-permute-start(bf16[2560,96]{0,1:T(8,128)(2,1)S(1)} %collective-permute-done.8), channel_id=1, source_target_pairs={{0,15},{1,0},{2,1},{3,2},{4,3},{5,4},{6,5},{7,6},{8,7},{9,8},{10,9... | collective-permute-start | bytes 1474568 | tf_op jit(solution)/shard_map/ppermute | solution.py:73
  71.9 6.1 %collective-permute-done.9 = bf16[2560,96]{0,1:T(8,128)(2,1)S(1)} collective-permute-done((bf16[2560,96]{0,1:T(8,128)(2,1)S(1)}, bf16[2560,96]{0,1:T(8,128)(2,1)S(1)}, u32[]{:S(2)}, u32[]{:S(2)}) %collective-permute-start.9) | collective-permute-done | bytes 491552 | tf_op jit(solution)/shard_map/ppermute | solution.py:70
  78.0 5.3 %collective-permute-start.12 = (bf16[2560,96]{0,1:T(8,128)(2,1)S(1)}, bf16[2560,96]{0,1:T(8,128)(2,1)S(1)}, u32[]{:S(2)}, u32[]{:S(2)}) collective-permute-start(bf16[2560,96]{0,1:T(8,128)(2,1)S(1)} %collective-permute-done.10), channel_id=1, source_target_pairs={{0,15},{1,0},{2,1},{3,2},{4,3},{5,4},{6,5},{7,6},{8,7},{9,8},{10,9... | collective-permute-start | bytes 1474568 | tf_op jit(solution)/shard_map/ppermute | solution.py:73
  85.0 5.3 %collective-permute-done.11 = bf16[2560,96]{0,1:T(8,128)(2,1)S(1)} collective-permute-done((bf16[2560,96]{0,1:T(8,128)(2,1)S(1)}, bf16[2560,96]{0,1:T(8,128)(2,1)S(1)}, u32[]{:S(2)}, u32[]{:S(2)}) %collective-permute-start.11) | collective-permute-done | bytes 491552 | tf_op jit(solution)/shard_map/ppermute | solution.py:70
  90.3 5.3 %collective-permute-start.14 = (bf16[2560,96]{0,1:T(8,128)(2,1)S(1)}, bf16[2560,96]{0,1:T(8,128)(2,1)S(1)}, u32[]{:S(2)}, u32[]{:S(2)}) collective-permute-start(bf16[2560,96]{0,1:T(8,128)(2,1)S(1)} %collective-permute-done.12), channel_id=1, source_target_pairs={{0,15},{1,0},{2,1},{3,2},{4,3},{5,4},{6,5},{7,6},{8,7},{9,8},{10,9... | collective-permute-start | bytes 1474568 | tf_op jit(solution)/shard_map/ppermute | solution.py:73
  97.3 5.4 %collective-permute-done.13 = bf16[2560,96]{0,1:T(8,128)(2,1)S(1)} collective-permute-done((bf16[2560,96]{0,1:T(8,128)(2,1)S(1)}, bf16[2560,96]{0,1:T(8,128)(2,1)S(1)}, u32[]{:S(2)}, u32[]{:S(2)}) %collective-permute-start.13) | collective-permute-done | bytes 491552 | tf_op jit(solution)/shard_map/ppermute | solution.py:70
  104.3 10.5 %collective-permute-done.15 = bf16[2560,96]{0,1:T(8,128)(2,1)S(1)} collective-permute-done((bf16[2560,96]{0,1:T(8,128)(2,1)S(1)}, bf16[2560,96]{0,1:T(8,128)(2,1)S(1)}, u32[]{:S(2)}, u32[]{:S(2)}) %collective-permute-start.15) | collective-permute-done | bytes 491552 | tf_op jit(solution)/shard_map/ppermute | solution.py:70
  115.7 12.2 %fusion.19 = bf16[1024,1536]{1,0:T(8,128)(2,1)S(1)} fusion(bf16[2560,1536]{0,1:T(8,128)(2,1)} %constant_dynamic-update-slice_fusion, bf16[512,2560]{1,0:T(8,128)(2,1)} %collective-permute-done, bf16[512,2560]{1,0:T(8,128)(2,1)} %fusion.13), kind=kOutput, calls=%fused_computation.27 | convolution fusion | flops 8065122304 | bytes 16252928 | tf_op jit(solution)/shard_map/dot_general | solution.py:81
  128.0 1.6 copy-done.2
  132.3 3.5 %all-to-all-start = ((s32[16,32,1]{1,2,0:T(1,128)}), s32[16,32,1]{1,2,0:T(1,128)S(1)}, u32[]{:S(2)}, u32[]{:S(2)}) async-start(s32[16,32,1]{1,2,0:T(1,128)} %all_to_all.20), calls=%async_computation | async-start | bytes 16384 | tf_op jit(solution)/shard_map/all_to_all | solution.py:91
  135.8 7.4 %all-to-all-done = s32[16,32,1]{1,2,0:T(1,128)S(1)} async-done(((s32[16,32,1]{1,2,0:T(1,128)}), s32[16,32,1]{1,2,0:T(1,128)S(1)}, u32[]{:S(2)}, u32[]{:S(2)}) %all-to-all-start) | async-done | bytes 2080 | tf_op jit(solution)/shard_map/all_to_all | solution.py:91
  143.2 1.5 broadcast_in_dim.55
  144.8 4.6 %all-to-all-start.3 = ((bf16[16,128,512]{2,1,0:T(8,128)(2,1)}), bf16[16,128,512]{2,1,0:T(8,128)(2,1)}, u32[]{:S(2)}, u32[]{:S(2)}) async-start(bf16[16,128,512]{2,1,0:T(8,128)(2,1)} %broadcast_in_dim.55), calls=%async_computation.3 | async-start | bytes 4194304 | tf_op jit(solution)/shard_map/all_to_all | solution.py:48
  149.4 2.1 broadcast_select_fusion.1
  151.5 1.6 copy.17
  153.1 1.6 copy.18
  154.7 2.2 pad_maximum_fusion
  156.9 7.8 %copy.19 = bf16[512,16,2,96]{3,2,1,0:T(2,128)(2,1)} copy(bf16[512,16,2,96]{0,3,1,2:T(8,128)(2,1)S(1)} %pad_maximum_fusion) | data formatting | bytes 6291456 | tf_op jit(solution)/shard_map/concatenate | solution.py:87
  164.7 12.4 %all_to_all.22 = bf16[16,32,3072]{2,1,0:T(8,128)(2,1)} reshape(bf16[512,16,2,96]{3,2,1,0:T(2,128)(2,1)} %copy.19) | data formatting | bytes 6291456 | tf_op jit(solution)/shard_map/all_to_all | solution.py:90
  177.1 3.5 %all-to-all-done.3 = bf16[16,128,512]{2,1,0:T(8,128)(2,1)} async-done(((bf16[16,128,512]{2,1,0:T(8,128)(2,1)}), bf16[16,128,512]{2,1,0:T(8,128)(2,1)}, u32[]{:S(2)}, u32[]{:S(2)}) %all-to-all-start.3) | async-done | bytes 2097184 | tf_op jit(solution)/shard_map/all_to_all | solution.py:48
  180.6 3.7 %all-to-all-start.1 = ((bf16[16,32,3072]{2,1,0:T(8,128)(2,1)}), bf16[16,32,3072]{2,1,0:T(8,128)(2,1)S(1)}, u32[]{:S(2)}, u32[]{:S(2)}) async-start(bf16[16,32,3072]{2,1,0:T(8,128)(2,1)} %all_to_all.22), calls=%async_computation.1 | async-start | bytes 6291456 | tf_op jit(solution)/shard_map/all_to_all | solution.py:90
  185.2 3.0 fusion.26
  188.2 42.2 %all-to-all-done.1 = bf16[16,32,3072]{2,1,0:T(8,128)(2,1)S(1)} async-done(((bf16[16,32,3072]{2,1,0:T(8,128)(2,1)}), bf16[16,32,3072]{2,1,0:T(8,128)(2,1)S(1)}, u32[]{:S(2)}, u32[]{:S(2)}) %all-to-all-start.1) | async-done | bytes 3145760 | tf_op jit(solution)/shard_map/all_to_all | solution.py:90
  230.4 1.8 convolution_convert_fusion
  232.4 2.6 copy.20
  235.0 3.4 %pad_maximum_fusion.1 = (bf16[2560,256]{1,0:T(8,128)(2,1)}, bf16[2560,256]{1,0:T(8,128)(2,1)}) fusion(bf16[512,256]{1,0:T(8,128)(2,1)S(1)} %get-tuple-element.91, bf16[2048,256]{1,0:T(8,128)(2,1)} %get-tuple-element.93, bf16[512,256]{1,0:T(8,128)(2,1)S(1)} %get-tuple-element.90, bf16[2048,256]{1,0:T(8,128)(2,1)} %get-tuple-element.92), kind=kLoop, calls=%fused_computation.31 | loop fusion | flops 5242880 | bytes 5242880 | tf_op jit(solution)/shard_map/concatenate | solution.py:20
  238.5 63.7 %while.11 = (s32[]{:T(128)}, bf16[10,512,256]{1,2,0:T(8,128)(2,1)S(1)}, bf16[10,512,256]{1,2,0:T(8,128)(2,1)}, bf16[2560,256]{1,0:T(8,128)(2,1)}, bf16[2560,256]...) while((s32[]{:T(128)}, bf16[10,512,256]{1,2,0:T(8,128)(2,1)S(1)}, ...), condition=%wide.region_4.5_spmd.clone, body=%wide.region_1.4_spmd.clone.sunk | while | flops 1357904896 | bytes 24394868 | solution.py:42
  238.5 3.7 %fusion.38 = (f32[512]{0:T(512)S(1)}, f32[512,2560]{1,0:T(8,128)S(1)}) fusion(bf16[2560,256]{1,0:T(8,128)(2,1)} %get-tuple-element.162, bf16[10,512,256]{1,2,0:T(8,128)(2,1)} %get-tuple-element.161, s32[]{:T(128)} %get-tuple-element.151, pred[2560]{0:T(1024)(128)(4,1)S(1)} %get-tuple-element.165, s32[512]{0:T(512)S(1)} %get-tuple-element.164), kind=kOutput, calls=%fused_computation.59.clone.1 | convolution fusion | flops 680263168 | bytes 6822912 | tf_op jit(solution)/shard_map/while/body/eval_jaxpr/dot_general | solution.py:35
  243.5 1.3 fusion.40
  244.8 3.7 %fusion.38 = (f32[512]{0:T(512)S(1)}, f32[512,2560]{1,0:T(8,128)S(1)}) fusion(bf16[2560,256]{1,0:T(8,128)(2,1)} %get-tuple-element.162, bf16[10,512,256]{1,2,0:T(8,128)(2,1)} %get-tuple-element.161, s32[]{:T(128)} %get-tuple-element.151, pred[2560]{0:T(1024)(128)(4,1)S(1)} %get-tuple-element.165, s32[512]{0:T(512)S(1)} %get-tuple-element.164), kind=kOutput, calls=%fused_computation.59.clone.1 | convolution fusion | flops 680263168 | bytes 6822912 | tf_op jit(solution)/shard_map/while/body/eval_jaxpr/dot_general | solution.py:35
  249.8 1.3 fusion.40
  251.2 3.7 %fusion.38 = (f32[512]{0:T(512)S(1)}, f32[512,2560]{1,0:T(8,128)S(1)}) fusion(bf16[2560,256]{1,0:T(8,128)(2,1)} %get-tuple-element.162, bf16[10,512,256]{1,2,0:T(8,128)(2,1)} %get-tuple-element.161, s32[]{:T(128)} %get-tuple-element.151, pred[2560]{0:T(1024)(128)(4,1)S(1)} %get-tuple-element.165, s32[512]{0:T(512)S(1)} %get-tuple-element.164), kind=kOutput, calls=%fused_computation.59.clone.1 | convolution fusion | flops 680263168 | bytes 6822912 | tf_op jit(solution)/shard_map/while/body/eval_jaxpr/dot_general | solution.py:35
  256.2 1.3 fusion.40
  257.6 3.7 %fusion.38 = (f32[512]{0:T(512)S(1)}, f32[512,2560]{1,0:T(8,128)S(1)}) fusion(bf16[2560,256]{1,0:T(8,128)(2,1)} %get-tuple-element.162, bf16[10,512,256]{1,2,0:T(8,128)(2,1)} %get-tuple-element.161, s32[]{:T(128)} %get-tuple-element.151, pred[2560]{0:T(1024)(128)(4,1)S(1)} %get-tuple-element.165, s32[512]{0:T(512)S(1)} %get-tuple-element.164), kind=kOutput, calls=%fused_computation.59.clone.1 | convolution fusion | flops 680263168 | bytes 6822912 | tf_op jit(solution)/shard_map/while/body/eval_jaxpr/dot_general | solution.py:35
  262.6 1.3 fusion.40
  263.9 3.7 %fusion.38 = (f32[512]{0:T(512)S(1)}, f32[512,2560]{1,0:T(8,128)S(1)}) fusion(bf16[2560,256]{1,0:T(8,128)(2,1)} %get-tuple-element.162, bf16[10,512,256]{1,2,0:T(8,128)(2,1)} %get-tuple-element.161, s32[]{:T(128)} %get-tuple-element.151, pred[2560]{0:T(1024)(128)(4,1)S(1)} %get-tuple-element.165, s32[512]{0:T(512)S(1)} %get-tuple-element.164), kind=kOutput, calls=%fused_computation.59.clone.1 | convolution fusion | flops 680263168 | bytes 6822912 | tf_op jit(solution)/shard_map/while/body/eval_jaxpr/dot_general | solution.py:35
  269.0 1.3 fusion.40
  270.3 3.7 %fusion.38 = (f32[512]{0:T(512)S(1)}, f32[512,2560]{1,0:T(8,128)S(1)}) fusion(bf16[2560,256]{1,0:T(8,128)(2,1)} %get-tuple-element.162, bf16[10,512,256]{1,2,0:T(8,128)(2,1)} %get-tuple-element.161, s32[]{:T(128)} %get-tuple-element.151, pred[2560]{0:T(1024)(128)(4,1)S(1)} %get-tuple-element.165, s32[512]{0:T(512)S(1)} %get-tuple-element.164), kind=kOutput, calls=%fused_computation.59.clone.1 | convolution fusion | flops 680263168 | bytes 6822912 | tf_op jit(solution)/shard_map/while/body/eval_jaxpr/dot_general | solution.py:35
  275.3 1.3 fusion.40
  276.7 3.7 %fusion.38 = (f32[512]{0:T(512)S(1)}, f32[512,2560]{1,0:T(8,128)S(1)}) fusion(bf16[2560,256]{1,0:T(8,128)(2,1)} %get-tuple-element.162, bf16[10,512,256]{1,2,0:T(8,128)(2,1)} %get-tuple-element.161, s32[]{:T(128)} %get-tuple-element.151, pred[2560]{0:T(1024)(128)(4,1)S(1)} %get-tuple-element.165, s32[512]{0:T(512)S(1)} %get-tuple-element.164), kind=kOutput, calls=%fused_computation.59.clone.1 | convolution fusion | flops 680263168 | bytes 6822912 | tf_op jit(solution)/shard_map/while/body/eval_jaxpr/dot_general | solution.py:35
  281.7 1.3 fusion.40
  283.0 3.7 %fusion.38 = (f32[512]{0:T(512)S(1)}, f32[512,2560]{1,0:T(8,128)S(1)}) fusion(bf16[2560,256]{1,0:T(8,128)(2,1)} %get-tuple-element.162, bf16[10,512,256]{1,2,0:T(8,128)(2,1)} %get-tuple-element.161, s32[]{:T(128)} %get-tuple-element.151, pred[2560]{0:T(1024)(128)(4,1)S(1)} %get-tuple-element.165, s32[512]{0:T(512)S(1)} %get-tuple-element.164), kind=kOutput, calls=%fused_computation.59.clone.1 | convolution fusion | flops 680263168 | bytes 6822912 | tf_op jit(solution)/shard_map/while/body/eval_jaxpr/dot_general | solution.py:35
  288.1 1.3 fusion.40
  289.4 3.7 %fusion.38 = (f32[512]{0:T(512)S(1)}, f32[512,2560]{1,0:T(8,128)S(1)}) fusion(bf16[2560,256]{1,0:T(8,128)(2,1)} %get-tuple-element.162, bf16[10,512,256]{1,2,0:T(8,128)(2,1)} %get-tuple-element.161, s32[]{:T(128)} %get-tuple-element.151, pred[2560]{0:T(1024)(128)(4,1)S(1)} %get-tuple-element.165, s32[512]{0:T(512)S(1)} %get-tuple-element.164), kind=kOutput, calls=%fused_computation.59.clone.1 | convolution fusion | flops 680263168 | bytes 6822912 | tf_op jit(solution)/shard_map/while/body/eval_jaxpr/dot_general | solution.py:35
  294.4 1.3 fusion.40
  295.8 3.7 %fusion.38 = (f32[512]{0:T(512)S(1)}, f32[512,2560]{1,0:T(8,128)S(1)}) fusion(bf16[2560,256]{1,0:T(8,128)(2,1)} %get-tuple-element.162, bf16[10,512,256]{1,2,0:T(8,128)(2,1)} %get-tuple-element.161, s32[]{:T(128)} %get-tuple-element.151, pred[2560]{0:T(1024)(128)(4,1)S(1)} %get-tuple-element.165, s32[512]{0:T(512)S(1)} %get-tuple-element.164), kind=kOutput, calls=%fused_computation.59.clone.1 | convolution fusion | flops 680263168 | bytes 6822912 | tf_op jit(solution)/shard_map/while/body/eval_jaxpr/dot_general | solution.py:35
  300.8 1.3 fusion.40
  302.1 1.5 copy-done.4
  303.6 2.2 fusion.18
  305.9 2.8 copy.23
  (95 shorter events, 29.1 us)
Async XLA Ops:
  0.0 8.6 %copy-start = (bf16[512,2560]{1,0:T(8,128)(2,1)S(1)}, bf16[512,2560]{1,0:T(8,128)(2,1)}, u32[]{:S(2)}) copy-start(bf16[512,2560]{1,0:T(8,128)(2,1)} %param.9) | copy-start | bytes 7864324
  0.0 1.4 copy-start.6
  0.0 9.2 %copy-start.8 = (f32[2560]{0:T(1024)S(1)}, f32[2560]{0:T(1024)}, u32[]{:S(2)}) copy-start(f32[2560]{0:T(1024)} %param.10) | copy-start | bytes 30724
  1.4 10.0 %copy-start.7 = (bf16[1,128,512]{2,1,0:T(8,128)(2,1)S(1)}, bf16[1,128,512]{2,1,0:T(8,128)(2,1)}, u32[]{:S(2)}) copy-start(bf16[1,128,512]{2,1,0:T(8,128)(2,1)} %param.12) | copy-start | bytes 393220
  2.2 9.1 %copy-start.1 = (bf16[2560,1536]{0,1:T(8,128)(2,1)}, bf16[2560,1536]{0,1:T(8,128)(2,1)S(1)}, u32[]{:S(2)}) copy-start(bf16[2560,1536]{0,1:T(8,128)(2,1)S(1)} %get-tuple-element.84) | copy-start | bytes 23592964
  2.2 17.9 %collective-permute-start.1 = (bf16[2560,96]{0,1:T(8,128)(2,1)}, bf16[2560,96]{0,1:T(8,128)(2,1)}, u32[]{:S(2)}, u32[]{:S(2)}) collective-permute-start(bf16[2560,96]{0,1:T(8,128)(2,1)} %get-tuple-element.85), channel_id=1, source_target_pairs={{0,1},{1,2},{2,3},{3,4},{4,5},{5,6},{6,7},{7,8},{8,9},{9,10},{10,1... | collective-permute-start | bytes 1474568 | tf_op jit(solution)/shard_map/ppermute | solution.py:70
  3.8 16.3 %collective-permute-start.2 = (bf16[2560,96]{0,1:T(8,128)(2,1)}, bf16[2560,96]{0,1:T(8,128)(2,1)S(1)}, u32[]{:S(2)}, u32[]{:S(2)}) collective-permute-start(bf16[2560,96]{0,1:T(8,128)(2,1)} %get-tuple-element.85), channel_id=1, source_target_pairs={{0,15},{1,0},{2,1},{3,2},{4,3},{5,4},{6,5},{7,6},{8,7},{9,8},{10,9... | collective-permute-start | bytes 1474568 | tf_op jit(solution)/shard_map/ppermute | solution.py:73
  11.3 104.3 %collective-permute-start = (bf16[512,2560]{1,0:T(8,128)(2,1)}, bf16[512,2560]{1,0:T(8,128)(2,1)}, u32[]{:S(2)}, u32[]{:S(2)}) collective-permute-start(bf16[512,2560]{1,0:T(8,128)(2,1)} %fusion.13), channel_id=1, source_target_pairs={{0,16},{16,0},{32,48},{48,32},{64,80},{80,64},{96,112},{112,96},{1... | collective-permute-start | bytes 7864328 | tf_op jit(solution)/shard_map/ppermute | solution.py:59
  12.4 119.9 %all-to-all-start.2 = ((bf16[8,128,512]{2,1,0:T(8,128)(2,1)}), bf16[8,128,512]{2,1,0:T(8,128)(2,1)S(1)}, u32[]{:S(2)}, u32[]{:S(2)}) async-start(bf16[8,128,512]{2,1,0:T(8,128)(2,1)} %broadcast_in_dim.53), calls=%async_computation.2 | async-start | bytes 2097152 | tf_op jit(solution)/shard_map/all_to_all | solution.py:48
  20.1 15.9 %collective-permute-start.3 = (bf16[2560,96]{0,1:T(8,128)(2,1)}, bf16[2560,96]{0,1:T(8,128)(2,1)S(1)}, u32[]{:S(2)}, u32[]{:S(2)}) collective-permute-start(bf16[2560,96]{0,1:T(8,128)(2,1)} %collective-permute-done.1), channel_id=1, source_target_pairs={{0,1},{1,2},{2,3},{3,4},{4,5},{5,6},{6,7},{7,8},{8,9},{9,10},{10,1... | collective-permute-start | bytes 1474568 | tf_op jit(solution)/shard_map/ppermute | solution.py:70
  20.1 15.9 %collective-permute-start.4 = (bf16[2560,96]{0,1:T(8,128)(2,1)S(1)}, bf16[2560,96]{0,1:T(8,128)(2,1)S(1)}, u32[]{:S(2)}, u32[]{:S(2)}) collective-permute-start(bf16[2560,96]{0,1:T(8,128)(2,1)S(1)} %collective-permute-done.2), channel_id=1, source_target_pairs={{0,15},{1,0},{2,1},{3,2},{4,3},{5,4},{6,5},{7,6},{8,7},{9,8},{10,9... | collective-permute-start | bytes 1474568 | tf_op jit(solution)/shard_map/ppermute | solution.py:73
  36.0 14.8 %collective-permute-start.5 = (bf16[2560,96]{0,1:T(8,128)(2,1)S(1)}, bf16[2560,96]{0,1:T(8,128)(2,1)S(1)}, u32[]{:S(2)}, u32[]{:S(2)}) collective-permute-start(bf16[2560,96]{0,1:T(8,128)(2,1)S(1)} %collective-permute-done.3), channel_id=1, source_target_pairs={{0,1},{1,2},{2,3},{3,4},{4,5},{5,6},{6,7},{7,8},{8,9},{9,10},{10,1... | collective-permute-start | bytes 1474568 | tf_op jit(solution)/shard_map/ppermute | solution.py:70
  36.0 14.8 %collective-permute-start.6 = (bf16[2560,96]{0,1:T(8,128)(2,1)S(1)}, bf16[2560,96]{0,1:T(8,128)(2,1)S(1)}, u32[]{:S(2)}, u32[]{:S(2)}) collective-permute-start(bf16[2560,96]{0,1:T(8,128)(2,1)S(1)} %collective-permute-done.4), channel_id=1, source_target_pairs={{0,15},{1,0},{2,1},{3,2},{4,3},{5,4},{6,5},{7,6},{8,7},{9,8},{10,9... | collective-permute-start | bytes 1474568 | tf_op jit(solution)/shard_map/ppermute | solution.py:73
  50.9 14.0 %collective-permute-start.7 = (bf16[2560,96]{0,1:T(8,128)(2,1)S(1)}, bf16[2560,96]{0,1:T(8,128)(2,1)S(1)}, u32[]{:S(2)}, u32[]{:S(2)}) collective-permute-start(bf16[2560,96]{0,1:T(8,128)(2,1)S(1)} %collective-permute-done.5), channel_id=1, source_target_pairs={{0,1},{1,2},{2,3},{3,4},{4,5},{5,6},{6,7},{7,8},{8,9},{9,10},{10,1... | collective-permute-start | bytes 1474568 | tf_op jit(solution)/shard_map/ppermute | solution.py:70
  50.9 14.0 %collective-permute-start.8 = (bf16[2560,96]{0,1:T(8,128)(2,1)S(1)}, bf16[2560,96]{0,1:T(8,128)(2,1)S(1)}, u32[]{:S(2)}, u32[]{:S(2)}) collective-permute-start(bf16[2560,96]{0,1:T(8,128)(2,1)S(1)} %collective-permute-done.6), channel_id=1, source_target_pairs={{0,15},{1,0},{2,1},{3,2},{4,3},{5,4},{6,5},{7,6},{8,7},{9,8},{10,9... | collective-permute-start | bytes 1474568 | tf_op jit(solution)/shard_map/ppermute | solution.py:73
  64.9 13.1 %collective-permute-start.9 = (bf16[2560,96]{0,1:T(8,128)(2,1)S(1)}, bf16[2560,96]{0,1:T(8,128)(2,1)S(1)}, u32[]{:S(2)}, u32[]{:S(2)}) collective-permute-start(bf16[2560,96]{0,1:T(8,128)(2,1)S(1)} %collective-permute-done.7), channel_id=1, source_target_pairs={{0,1},{1,2},{2,3},{3,4},{4,5},{5,6},{6,7},{7,8},{8,9},{9,10},{10,1... | collective-permute-start | bytes 1474568 | tf_op jit(solution)/shard_map/ppermute | solution.py:70
  64.9 13.1 %collective-permute-start.10 = (bf16[2560,96]{0,1:T(8,128)(2,1)S(1)}, bf16[2560,96]{0,1:T(8,128)(2,1)S(1)}, u32[]{:S(2)}, u32[]{:S(2)}) collective-permute-start(bf16[2560,96]{0,1:T(8,128)(2,1)S(1)} %collective-permute-done.8), channel_id=1, source_target_pairs={{0,15},{1,0},{2,1},{3,2},{4,3},{5,4},{6,5},{7,6},{8,7},{9,8},{10,9... | collective-permute-start | bytes 1474568 | tf_op jit(solution)/shard_map/ppermute | solution.py:73
  78.0 12.3 %collective-permute-start.11 = (bf16[2560,96]{0,1:T(8,128)(2,1)S(1)}, bf16[2560,96]{0,1:T(8,128)(2,1)S(1)}, u32[]{:S(2)}, u32[]{:S(2)}) collective-permute-start(bf16[2560,96]{0,1:T(8,128)(2,1)S(1)} %collective-permute-done.9), channel_id=1, source_target_pairs={{0,1},{1,2},{2,3},{3,4},{4,5},{5,6},{6,7},{7,8},{8,9},{9,10},{10,1... | collective-permute-start | bytes 1474568 | tf_op jit(solution)/shard_map/ppermute | solution.py:70
  78.0 12.3 %collective-permute-start.12 = (bf16[2560,96]{0,1:T(8,128)(2,1)S(1)}, bf16[2560,96]{0,1:T(8,128)(2,1)S(1)}, u32[]{:S(2)}, u32[]{:S(2)}) collective-permute-start(bf16[2560,96]{0,1:T(8,128)(2,1)S(1)} %collective-permute-done.10), channel_id=1, source_target_pairs={{0,15},{1,0},{2,1},{3,2},{4,3},{5,4},{6,5},{7,6},{8,7},{9,8},{10,9... | collective-permute-start | bytes 1474568 | tf_op jit(solution)/shard_map/ppermute | solution.py:73
  90.3 12.4 %collective-permute-start.13 = (bf16[2560,96]{0,1:T(8,128)(2,1)S(1)}, bf16[2560,96]{0,1:T(8,128)(2,1)S(1)}, u32[]{:S(2)}, u32[]{:S(2)}) collective-permute-start(bf16[2560,96]{0,1:T(8,128)(2,1)S(1)} %collective-permute-done.11), channel_id=1, source_target_pairs={{0,1},{1,2},{2,3},{3,4},{4,5},{5,6},{6,7},{7,8},{8,9},{9,10},{10,1... | collective-permute-start | bytes 1474568 | tf_op jit(solution)/shard_map/ppermute | solution.py:70
  90.3 13.2 %collective-permute-start.14 = (bf16[2560,96]{0,1:T(8,128)(2,1)S(1)}, bf16[2560,96]{0,1:T(8,128)(2,1)S(1)}, u32[]{:S(2)}, u32[]{:S(2)}) collective-permute-start(bf16[2560,96]{0,1:T(8,128)(2,1)S(1)} %collective-permute-done.12), channel_id=1, source_target_pairs={{0,15},{1,0},{2,1},{3,2},{4,3},{5,4},{6,5},{7,6},{8,7},{9,8},{10,9... | collective-permute-start | bytes 1474568 | tf_op jit(solution)/shard_map/ppermute | solution.py:73
  102.7 12.2 %collective-permute-start.15 = (bf16[2560,96]{0,1:T(8,128)(2,1)S(1)}, bf16[2560,96]{0,1:T(8,128)(2,1)S(1)}, u32[]{:S(2)}, u32[]{:S(2)}) collective-permute-start(bf16[2560,96]{0,1:T(8,128)(2,1)S(1)} %collective-permute-done.13), channel_id=1, source_target_pairs={{0,1},{1,2},{2,3},{3,4},{4,5},{5,6},{6,7},{7,8},{8,9},{9,10},{10,1... | collective-permute-start | bytes 1474568 | tf_op jit(solution)/shard_map/ppermute | solution.py:70
  115.7 14.6 %copy-start.9 = (s32[1,512]{1,0:T(1,128)S(1)}, s32[1,512]{1,0:T(1,128)}, u32[]{:S(2)}) copy-start(s32[1,512]{1,0:T(1,128)} %param.15) | copy-start | bytes 6148
  127.9 1.6 copy-start.2
  129.7 19.7 %collective-permute-start.16 = (bf16[512,1536]{1,0:T(8,128)(2,1)S(1)}, bf16[512,1536]{1,0:T(8,128)(2,1)}, u32[]{:S(2)}, u32[]{:S(2)}) collective-permute-start(bf16[512,1536]{1,0:T(8,128)(2,1)S(1)} %slice.32), channel_id=1, source_target_pairs={{0,16},{16,0},{32,48},{48,32},{64,80},{80,64},{96,112},{112,96},{1... | collective-permute-start | bytes 4718600 | tf_op jit(solution)/shard_map/ppermute | solution.py:83
  132.3 10.9 %all-to-all-start = ((s32[16,32,1]{1,2,0:T(1,128)}), s32[16,32,1]{1,2,0:T(1,128)S(1)}, u32[]{:S(2)}, u32[]{:S(2)}) async-start(s32[16,32,1]{1,2,0:T(1,128)} %all_to_all.20), calls=%async_computation | async-start | bytes 16384 | tf_op jit(solution)/shard_map/all_to_all | solution.py:91
  144.8 35.9 %all-to-all-start.3 = ((bf16[16,128,512]{2,1,0:T(8,128)(2,1)}), bf16[16,128,512]{2,1,0:T(8,128)(2,1)}, u32[]{:S(2)}, u32[]{:S(2)}) async-start(bf16[16,128,512]{2,1,0:T(8,128)(2,1)} %broadcast_in_dim.55), calls=%async_computation.3 | async-start | bytes 4194304 | tf_op jit(solution)/shard_map/all_to_all | solution.py:48
  180.6 49.7 %all-to-all-start.1 = ((bf16[16,32,3072]{2,1,0:T(8,128)(2,1)}), bf16[16,32,3072]{2,1,0:T(8,128)(2,1)S(1)}, u32[]{:S(2)}, u32[]{:S(2)}) async-start(bf16[16,32,3072]{2,1,0:T(8,128)(2,1)} %all_to_all.22), calls=%async_computation.1 | async-start | bytes 6291456 | tf_op jit(solution)/shard_map/all_to_all | solution.py:90
  235.0 3.4 %copy-start.3 = (bf16[10,512,256]{1,2,0:T(8,128)(2,1)S(1)}, bf16[10,512,256]{1,2,0:T(8,128)(2,1)}, u32[]{:S(2)}) copy-start(bf16[10,512,256]{1,2,0:T(8,128)(2,1)} %custom-call) | copy-start | bytes 7864324
  242.2 1.3 copy-start.5
  248.5 1.3 copy-start.5
  254.9 1.3 copy-start.5
  261.3 1.3 copy-start.5
  267.6 1.3 copy-start.5
  274.0 1.3 copy-start.5
  280.4 1.3 copy-start.5
  286.7 1.3 copy-start.5
  293.1 1.3 copy-start.5
  299.5 1.3 copy-start.5
  302.1 1.5 copy-start.4
